TPU v7x, 128 devices: a whole 4x4x4 slice. The times are simulated.
128 devices in a mesh: expert: 32 (over y, z, core), dp: 4 (over x).
Axes of the slice: x: 4, y: 4, z: 4, core: 2. Of those that a mesh axis runs over, the one named last changes fastest.
Arguments:
- activations: bfloat16 [2048, 7168], P(('expert', 'dp')), may hold values from -6 to 6
- cotangent: bfloat16 [2048, 7168], P(('expert', 'dp')), may hold values from -6 to 6
- route_ids: int32 [2048, 8], P(('expert', 'dp')), may hold values from 0 to 31, all different within a row; in each aligned block of 16 rows (0 to 15, 16 to 31, ...) at most 5 rows name the same one
- route_weights: float32 [2048, 8], P(('expert', 'dp')), may hold values from 0.05 to 0.6
- gate_weights: bfloat16 [32, 7168, 1024], P('expert', 'dp'), may hold values from -0.0625 to 0.0625
- up_weights: bfloat16 [32, 7168, 1024], P('expert', 'dp'), may hold values from -0.0625 to 0.0625
- down_weights: bfloat16 [32, 1024, 7168], P('expert', None, 'dp'), may hold values from -0.1875 to 0.1875
Outputs:
- grad_input: bfloat16 [2048, 7168], P(('expert', 'dp'))
- grad_gate: bfloat16 [32, 7168, 1024], P('expert', 'dp')
- grad_up: bfloat16 [32, 7168, 1024], P('expert', 'dp')
- grad_down: bfloat16 [32, 1024, 7168], P('expert', None, 'dp')
Inputs may be any that keep to these rules, and one draw needn't show every extreme that they name: `route_ids`: each token names 8 different experts. Among the routes of one device's 16 tokens, no expert is named more than 5 times, a bound that some block reaches.
All inputs are finite; a program needn't handle non-finite values.
Results may differ from a plain program's by a relative error of at most 0.0064.
Values may be sent and summed in bfloat16 or wider, within the bound.
No kernel may reach another device: no remote copies, remote signals or barrier semaphores. Data moves between devices by JAX's collectives and lax.ppermute only.
A program may use at most 128 MiB of HBM per device.

v0:
```python
import jax
import jax.numpy as jnp
from jax import lax
from jax.sharding import PartitionSpec as P


def swiglu_back(gate, upper, upstream):
    sigma = jax.nn.sigmoid(gate)
    silu_gate = gate * sigma
    activated = (silu_gate * upper).astype(jnp.bfloat16)
    grad_pre = (upstream * upper * sigma * (1.0 + gate * (1.0 - sigma))).astype(jnp.bfloat16)
    grad_lin = (upstream * silu_gate).astype(jnp.bfloat16)
    return (grad_pre, grad_lin, activated)


def contract_rows(left, right):
    return lax.dot_general(
        left, right, (((0,), (0,)), ((), ())), preferred_element_type=jnp.float32
    )


def exchange(parts, num_dp):
    rows, cols = parts.shape
    parts = parts.reshape(num_dp, rows // num_dp, cols)
    me = lax.axis_index("dp")
    summed = lax.dynamic_index_in_dim(parts, me, 0, keepdims=False)
    for shift in range(1, num_dp):
        block = lax.dynamic_index_in_dim(parts, (me + shift) % num_dp, 0, keepdims=False)
        pairs = [(i, (i + shift) % num_dp) for i in range(num_dp)]
        came = lax.ppermute(block.astype(jnp.bfloat16), "dp", pairs)
        summed = summed + came.astype(jnp.float32)
    return summed


def shards(
    activations, cotangent, route_ids, route_weights, gate_weights, up_weights, down_weights
):
    tok_rows, width = activations.shape
    topk = route_ids.shape[1]
    num_dp = lax.axis_size("dp")
    num_exp = lax.axis_size("expert")
    slice_width = gate_weights.shape[1]
    hidden = gate_weights.shape[2]
    capacity = min(tok_rows, 5 * tok_rows * topk // (4 * num_exp))
    flat_ids = route_ids.reshape(-1)
    expert_iota = jnp.arange(num_exp, dtype=jnp.int32)
    onehot = (flat_ids[:, None] == expert_iota[None, :]).astype(jnp.int32)
    before = jnp.cumsum(onehot, axis=0) - onehot
    slot = jnp.sum(before * onehot, axis=1)
    target = (flat_ids * capacity + slot).reshape(tok_rows, topk)
    slot_iota = jnp.arange(num_exp * capacity, dtype=jnp.int32)
    matches = target[:, :, None] == slot_iota[None, None, :]
    placing = jnp.any(matches, axis=1).astype(jnp.bfloat16)
    slot_weight = jnp.sum(jnp.where(matches, route_weights[:, :, None], 0.0), axis=(0, 1))
    by_slice = lambda a: jnp.swapaxes(a.reshape(tok_rows, num_dp, slice_width), 0, 1)
    both = jnp.concatenate([by_slice(activations), by_slice(cotangent)], axis=2)
    slots = placing.T.reshape(num_exp, capacity, tok_rows)
    scale = slot_weight.reshape(num_exp, capacity)
    gate_local = gate_weights[0]
    up_local = up_weights[0]
    down_local = down_weights[0]
    axes = ("dp", "expert")
    split = (capacity + 1) // 2
    bounds = [(0, split), (split, capacity)]
    kept = []
    pieces = []
    for lo, hi in bounds:
        take = hi - lo
        rows = num_exp * take
        pick = jnp.broadcast_to(
            slots[:, lo:hi].reshape(1, rows, tok_rows), (num_dp, rows, tok_rows)
        )
        gathered_rows = lax.dot_general(
            pick, both, (((2,), (1,)), ((0,), (0,))), preferred_element_type=jnp.float32
        )
        weight = jnp.concatenate(
            [
                jnp.ones((rows, slice_width), jnp.float32),
                jnp.broadcast_to(scale[:, lo:hi].reshape(rows, 1), (rows, slice_width)),
            ],
            axis=1,
        )
        flat_both = (gathered_rows * weight[None]).astype(jnp.bfloat16)
        flat_both = flat_both.reshape(num_dp * num_exp, take, 2 * slice_width)
        recv_both = lax.all_to_all(flat_both, axes, split_axis=0, concat_axis=0, tiled=True)
        recv_both = recv_both.reshape(num_exp * num_dp * take, 2 * slice_width)
        act_rows = recv_both[:, :slice_width]
        cot_rows = recv_both[:, slice_width:]
        gate_part = jnp.dot(act_rows, gate_local, preferred_element_type=jnp.float32)
        up_part = jnp.dot(act_rows, up_local, preferred_element_type=jnp.float32)
        back_part = lax.dot_general(
            cot_rows, down_local, (((1,), (1,)), ((), ())), preferred_element_type=jnp.float32
        )
        summed = exchange(jnp.concatenate([gate_part, up_part, back_part], axis=1), num_dp)
        grad_pre, grad_lin, activated = swiglu_back(
            summed[:, :hidden], summed[:, hidden : 2 * hidden], summed[:, 2 * hidden :]
        )
        gathered = lax.all_gather(
            jnp.concatenate([grad_pre, grad_lin, activated], axis=1), "dp", axis=0, tiled=True
        )
        grad_pre = gathered[:, :hidden]
        grad_lin = gathered[:, hidden : 2 * hidden]
        activated = gathered[:, 2 * hidden :]
        rows_back = lax.dot_general(
            grad_pre, gate_local, (((1,), (1,)), ((), ())), preferred_element_type=jnp.float32
        ) + lax.dot_general(
            grad_lin, up_local, (((1,), (1,)), ((), ())), preferred_element_type=jnp.float32
        )
        kept.append((act_rows, cot_rows, grad_pre, grad_lin, activated))
        flat_back = rows_back.astype(jnp.bfloat16).reshape(num_dp * num_exp, take, slice_width)
        arrived = lax.all_to_all(flat_back, axes, split_axis=0, concat_axis=0, tiled=True)
        pieces.append(arrived.reshape(num_dp, num_exp, take, slice_width))
    act_all, cot_all, pre_all, lin_all, activated_all = (
        jnp.concatenate(group, axis=0) for group in zip(*kept)
    )
    grad_gate = contract_rows(act_all, pre_all).astype(jnp.bfloat16)[None]
    grad_up = contract_rows(act_all, lin_all).astype(jnp.bfloat16)[None]
    grad_down = contract_rows(activated_all, cot_all).astype(jnp.bfloat16)[None]
    arrived = jnp.concatenate(pieces, axis=2).reshape(num_dp, num_exp * capacity, slice_width)
    spread = jnp.broadcast_to(placing[None], (num_dp,) + placing.shape)
    grad_slices = lax.dot_general(
        spread, arrived, (((2,), (1,)), ((0,), (0,))), preferred_element_type=jnp.float32
    ).astype(jnp.bfloat16)
    grad_input = jnp.swapaxes(grad_slices, 0, 1).reshape(tok_rows, width)
    return (grad_input, grad_gate, grad_up, grad_down)


def solution(mesh):
    placed = (
        P(("expert", "dp"), None),
        P(("expert", "dp"), None),
        P(("expert", "dp"), None),
        P(("expert", "dp"), None),
        P("expert", "dp", None),
        P("expert", "dp", None),
        P("expert", None, "dp"),
    )
    return jax.shard_map(
        shards,
        mesh=mesh,
        in_specs=placed,
        out_specs=(
            P(("expert", "dp"), None),
            P("expert", "dp", None),
            P("expert", "dp", None),
            P("expert", None, "dp"),
        ),
        check_vma=False,
    )
```

profile of v0, /device:TPU:1, one launch (start us, length us, event | category | flops | bytes accessed | tf_op | source)
XLA Modules:
  0.0 270.5 jit_solution(9096746041630390274)
XLA Ops:
  7.2 0.8 copy.51
  11.1 1.6 reshape.97
  12.8 11.9 %all-to-all-start.2 = ((bf16[128,2,3584]{2,1,0:T(2,128)(2,1)}), bf16[128,2,3584]{2,1,0:T(2,128)(2,1)}, u32[]{:S(2)}, u32[]{:S(2)}) async-start(bf16[128,2,3584]{2,1,0:T(2,128)(2,1)} %reshape.97), calls=%async_computation.2 | async-start | bytes 3670016 | tf_op jit(solution)/shard_map/all_to_all | solution.py:85
  25.2 0.9 fusion
  26.1 4.0 %reshape.92 = bf16[128,3,3584]{2,1,0:T(4,128)(2,1)} reshape(bf16[4,96,3584]{2,1,0:T(8,128)(2,1)S(1)} %fusion) | data formatting | bytes 5505024 | tf_op jit(solution)/shard_map/reshape | solution.py:84
  30.2 21.8 %all-to-all-done.2 = bf16[128,2,3584]{2,1,0:T(2,128)(2,1)} async-done(((bf16[128,2,3584]{2,1,0:T(2,128)(2,1)}), bf16[128,2,3584]{2,1,0:T(2,128)(2,1)}, u32[]{:S(2)}, u32[]{:S(2)}) %all-to-all-start.2) | async-done | bytes 1835040 | tf_op jit(solution)/shard_map/all_to_all | solution.py:85
  52.0 5.7 %all-to-all-start = ((bf16[128,3,3584]{2,1,0:T(4,128)(2,1)}), bf16[128,3,3584]{2,1,0:T(4,128)(2,1)}, u32[]{:S(2)}, u32[]{:S(2)}) async-start(bf16[128,3,3584]{2,1,0:T(4,128)(2,1)} %reshape.92), calls=%async_computation | async-start | bytes 7340032 | tf_op jit(solution)/shard_map/all_to_all | solution.py:85
  57.8 4.1 %reshape.98 = bf16[256,3584]{1,0:T(8,128)(2,1)S(1)} reshape(bf16[128,2,3584]{2,1,0:T(2,128)(2,1)} %all-to-all-done.2) | data formatting | bytes 3670016 | tf_op jit(solution)/shard_map/reshape | solution.py:86
  61.9 3.8 %fusion.8 = f32[256,1024]{1,0:T(8,128)S(1)} fusion(bf16[1,1792,1024]{2,1,0:T(8,128)(2,1)} %param.12, bf16[256,3584]{1,0:T(8,128)(2,1)S(1)} %reshape.98), kind=kOutput, calls=%fused_computation.14 | convolution fusion | flops 939524096 | bytes 5636096 | tf_op jit(solution)/shard_map/dot_general | solution.py:90
  65.7 1.1 fusion.2
  66.9 0.9 copy-done.11
  67.8 1.1 fusion.16
  69.1 1.0 fusion.60
  70.1 1.4 collective-permute-start.3
  71.5 1.3 collective-permute-start.5
  72.8 1.7 collective-permute-start.4
  74.5 33.5 %collective-permute-done.3 = bf16[64,3072]{1,0:T(8,128)(2,1)} collective-permute-done((bf16[64,3072]{1,0:T(8,128)(2,1)}, bf16[64,3072]{1,0:T(8,128)(2,1)}, u32[]{:S(2)}, u32[]{:S(2)}) %collective-permute-start.3) | collective-permute-done | bytes 393248 | tf_op jit(solution)/shard_map/ppermute | solution.py:30
  108.0 8.5 %collective-permute-done.4 = bf16[64,3072]{1,0:T(8,128)(2,1)} collective-permute-done((bf16[64,3072]{1,0:T(8,128)(2,1)S(1)}, bf16[64,3072]{1,0:T(8,128)(2,1)}, u32[]{:S(2)}, u32[]{:S(2)}) %collective-permute-start.4) | collective-permute-done | bytes 393248 | tf_op jit(solution)/shard_map/ppermute | solution.py:30
  116.5 1.4 fusion.56
  118.0 0.8 pad_maximum_fusion.8
  119.1 5.6 %reshape.93 = bf16[384,3584]{1,0:T(8,128)(2,1)S(1)} reshape(bf16[128,3,3584]{2,1,0:T(4,128)(2,1)} %all-to-all-done) | data formatting | bytes 5505024 | tf_op jit(solution)/shard_map/reshape | solution.py:86
  124.7 3.8 %fusion.12 = f32[384,1024]{1,0:T(8,128)S(1)} fusion(bf16[1,1792,1024]{2,1,0:T(8,128)(2,1)} %param.12, bf16[384,3584]{1,0:T(8,128)(2,1)S(1)} %reshape.93), kind=kOutput, calls=%fused_computation.18 | convolution fusion | flops 1409286144 | bytes 6619136 | tf_op jit(solution)/shard_map/dot_general | solution.py:90
  128.5 1.6 fusion.4
  130.8 1.7 fusion.20
  133.6 2.4 collective-permute-start.2
  136.0 21.8 %collective-permute-done = bf16[96,3072]{1,0:T(8,128)(2,1)S(1)} collective-permute-done((bf16[96,3072]{1,0:T(8,128)(2,1)S(1)}, bf16[96,3072]{1,0:T(8,128)(2,1)S(1)}, u32[]{:S(2)}, u32[]{:S(2)}) %collective-permute-start) | collective-permute-done | bytes 589856 | tf_op jit(solution)/shard_map/ppermute | solution.py:30
  157.7 12.9 %collective-permute-done.1 = bf16[96,3072]{1,0:T(8,128)(2,1)S(1)} collective-permute-done((bf16[96,3072]{1,0:T(8,128)(2,1)S(1)}, bf16[96,3072]{1,0:T(8,128)(2,1)S(1)}, u32[]{:S(2)}, u32[]{:S(2)}) %collective-permute-start.1) | collective-permute-done | bytes 589856 | tf_op jit(solution)/shard_map/ppermute | solution.py:30
  171.2 0.9 pad_maximum_fusion.6
  172.1 2.8 %fusion.87 = (bf16[256,1792]{1,0:T(8,128)(2,1)}, bf16[256,1792]{1,0:T(8,128)(2,1)}) fusion(bf16[256,3584]{1,0:T(8,128)(2,1)} %copy-done), kind=kLoop, calls=%fused_computation.114 | loop fusion | bytes 3670016 | tf_op jit(solution)/shard_map/slice | solution.py:88
  174.9 1.7 fusion.85
  176.6 3.5 %fusion.6 = f32[256,1792]{1,0:T(8,128)S(1)} fusion(bf16[1,1792,1024]{2,1,0:T(8,128)(2,1)} %param.12, bf16[256,3072]{1,0:T(8,128)(2,1)} %all-gather.5.cloned.1.call-done), kind=kOutput, calls=%fused_computation.12 | convolution fusion | flops 939524096 | bytes 6029312 | tf_op jit(solution)/shard_map/dot_general | solution.py:106
  180.1 2.2 fusion.34
  182.3 1.3 reshape.100
  183.6 8.1 %all-to-all-start.3 = ((bf16[128,2,1792]{2,1,0:T(2,128)(2,1)}), bf16[128,2,1792]{2,1,0:T(2,128)(2,1)S(1)}, u32[]{:S(2)}, u32[]{:S(2)}) async-start(bf16[128,2,1792]{2,1,0:T(2,128)(2,1)} %reshape.100), calls=%async_computation.3 | async-start | bytes 1835008 | tf_op jit(solution)/shard_map/all_to_all | solution.py:111
  191.7 22.7 %all-gather.3.cloned.1.call-done = bf16[384,3072]{1,0:T(8,128)(2,1)} async-done(((bf16[96,3072]{1,0:T(8,128)(2,1)}), bf16[384,3072]{1,0:T(8,128)(2,1)}) %all-gather.3.cloned.1.call-update) | async-done | bytes 2359312 | tf_op jit(solution)/shard_map/all_gather | solution.py:98
  214.4 4.1 %fusion.10 = f32[384,1792]{1,0:T(8,128)S(1)} fusion(bf16[1,1792,1024]{2,1,0:T(8,128)(2,1)} %param.12, bf16[384,3072]{1,0:T(8,128)(2,1)} %all-gather.3.cloned.1.call-done), kind=kOutput, calls=%fused_computation.16 | convolution fusion | flops 1409286144 | bytes 7208960 | tf_op jit(solution)/shard_map/dot_general | solution.py:106
  218.4 2.8 %fusion.28 = bf16[384,1792]{1,0:T(8,128)(2,1)S(1)} fusion(f32[384,1792]{1,0:T(8,128)S(1)} %fusion.10, bf16[1,1792,1024]{2,1,0:T(8,128)(2,1)S(1)} %copy-done.14, bf16[384,3072]{1,0:T(8,128)(2,1)} %all-gather.3.cloned.1.call-done), kind=kOutput, calls=%fused_computation.33 | convolution fusion | flops 1410662400 | bytes 8585216 | tf_op jit(solution)/shard_map/dot_general | solution.py:104
  221.3 2.1 reshape.95
  223.3 8.8 %all-to-all-start.1 = ((bf16[128,3,1792]{2,1,0:T(4,128)(2,1)}), bf16[128,3,1792]{2,1,0:T(4,128)(2,1)S(1)}, u32[]{:S(2)}, u32[]{:S(2)}) async-start(bf16[128,3,1792]{2,1,0:T(4,128)(2,1)} %reshape.95), calls=%async_computation.1 | async-start | bytes 3670016 | tf_op jit(solution)/shard_map/all_to_all | solution.py:111
  232.1 1.6 fusion.88
  233.8 1.7 copy.61
  235.7 1.1 copy-done.4
  237.0 4.5 %fusion.23 = bf16[1,1792,1024]{2,1,0:T(8,128)(2,1)} fusion(bf16[256,1792]{1,0:T(8,128)(2,1)S(1)} %copy-done.6, bf16[384,1792]{1,0:T(8,128)(2,1)S(1)} %copy-done.4, bf16[256,1024]{1,0:T(8,128)(2,1)S(1)} %get-tuple-element.18, bf16[384,1024]{1,0:T(8,128)(2,1)S(1)} %get-tuple-element.13), kind=kOutput, calls=%fused_computation.29 | convolution fusion | flops 2357854208 | bytes 7274496 | tf_op jit(solution)/shard_map/dot_general | solution.py:17
  241.6 4.5 %fusion.22 = bf16[1,1792,1024]{2,1,0:T(8,128)(2,1)} fusion(bf16[256,1792]{1,0:T(8,128)(2,1)S(1)} %copy-done.6, bf16[384,1792]{1,0:T(8,128)(2,1)S(1)} %copy-done.4, bf16[256,1024]{1,0:T(8,128)(2,1)S(1)} %get-tuple-element.19, bf16[384,1024]{1,0:T(8,128)(2,1)S(1)} %get-tuple-element.14), kind=kOutput, calls=%fused_computation.28 | convolution fusion | flops 2357854208 | bytes 7274496 | tf_op jit(solution)/shard_map/dot_general | solution.py:17
  246.1 4.5 %fusion.24 = bf16[1,1024,1792]{2,1,0:T(8,128)(2,1)} fusion(bf16[256,1792]{1,0:T(8,128)(2,1)S(1)} %copy-done.5, bf16[384,1792]{1,0:T(8,128)(2,1)S(1)} %copy-done.3, bf16[256,1024]{1,0:T(8,128)(2,1)S(1)} %get-tuple-element.17, bf16[384,1024]{1,0:T(8,128)(2,1)S(1)} %get-tuple-element.12), kind=kOutput, calls=%fused_computation.30 | convolution fusion | flops 2357854208 | bytes 7274496 | tf_op jit(solution)/shard_map/dot_general | solution.py:17
  250.6 9.1 %all-to-all-done.1 = bf16[128,3,1792]{2,1,0:T(4,128)(2,1)S(1)} async-done(((bf16[128,3,1792]{2,1,0:T(4,128)(2,1)}), bf16[128,3,1792]{2,1,0:T(4,128)(2,1)S(1)}, u32[]{:S(2)}, u32[]{:S(2)}) %all-to-all-start.1) | async-done | bytes 1376288 | tf_op jit(solution)/shard_map/all_to_all | solution.py:111
  259.7 1.3 copy.60
  261.1 1.5 pad_maximum_fusion.2
  (75 shorter events, 8.1 us)
Async XLA Ops:
  7.2 3.2 %copy-start.7 = (bf16[16,7168]{1,0:T(8,128)(2,1)S(1)}, bf16[16,7168]{1,0:T(8,128)(2,1)}, u32[]{:S(2)}) copy-start(bf16[16,7168]{1,0:T(8,128)(2,1)} %param.8) | copy-start | bytes 688132
  7.2 3.2 %copy-start.8 = (bf16[16,7168]{1,0:T(8,128)(2,1)S(1)}, bf16[16,7168]{1,0:T(8,128)(2,1)}, u32[]{:S(2)}) copy-start(bf16[16,7168]{1,0:T(8,128)(2,1)} %param.7) | copy-start | bytes 688132
  12.8 39.2 %all-to-all-start.2 = ((bf16[128,2,3584]{2,1,0:T(2,128)(2,1)}), bf16[128,2,3584]{2,1,0:T(2,128)(2,1)}, u32[]{:S(2)}, u32[]{:S(2)}) async-start(bf16[128,2,3584]{2,1,0:T(2,128)(2,1)} %reshape.97), calls=%async_computation.2 | async-start | bytes 3670016 | tf_op jit(solution)/shard_map/all_to_all | solution.py:85
  52.0 67.1 %all-to-all-start = ((bf16[128,3,3584]{2,1,0:T(4,128)(2,1)}), bf16[128,3,3584]{2,1,0:T(4,128)(2,1)}, u32[]{:S(2)}, u32[]{:S(2)}) async-start(bf16[128,3,3584]{2,1,0:T(4,128)(2,1)} %reshape.92), calls=%async_computation | async-start | bytes 7340032 | tf_op jit(solution)/shard_map/all_to_all | solution.py:85
  57.7 118.8 %all-gather.5.cloned.1.call-start = ((), (), s32[]{:S(2)}) async-start(), calls=%async_computation.5 | async-start | bytes 1966080 | tf_op jit(solution)/shard_map/all_gather | solution.py:98
  61.8 5.0 %copy-start = (bf16[256,3584]{1,0:T(8,128)(2,1)}, bf16[256,3584]{1,0:T(8,128)(2,1)S(1)}, u32[]{:S(2)}) copy-start(bf16[256,3584]{1,0:T(8,128)(2,1)S(1)} %reshape.98) | copy-start | bytes 5505028
  61.9 3.9 %copy-start.9 = (bf16[1,1024,1792]{2,1,0:T(8,128)(2,1)S(1)}, bf16[1,1024,1792]{2,1,0:T(8,128)(2,1)}, u32[]{:S(2)}) copy-start(bf16[1,1024,1792]{2,1,0:T(8,128)(2,1)} %param.13) | copy-start | bytes 11010052
  65.7 2.0 copy-start.11
  70.1 37.8 %collective-permute-start.3 = (bf16[64,3072]{1,0:T(8,128)(2,1)}, bf16[64,3072]{1,0:T(8,128)(2,1)}, u32[]{:S(2)}, u32[]{:S(2)}) collective-permute-start(bf16[64,3072]{1,0:T(8,128)(2,1)} %get-tuple-element.7), channel_id=1, source_target_pairs={{0,1},{1,2},{2,3},{3,0},{4,5},{5,6},{6,7},{7,4},{8,9},{9,10},{10,1... | collective-permute-start | bytes 1179656 | tf_op jit(solution)/shard_map/ppermute | solution.py:30
  71.5 36.5 %collective-permute-start.5 = (bf16[64,3072]{1,0:T(8,128)(2,1)}, bf16[64,3072]{1,0:T(8,128)(2,1)}, u32[]{:S(2)}, u32[]{:S(2)}) collective-permute-start(bf16[64,3072]{1,0:T(8,128)(2,1)} %get-tuple-element.8), channel_id=1, source_target_pairs={{0,3},{1,0},{2,1},{3,2},{4,7},{5,4},{6,5},{7,6},{8,11},{9,8},{10,9... | collective-permute-start | bytes 1179656 | tf_op jit(solution)/shard_map/ppermute | solution.py:30
  72.8 43.7 %collective-permute-start.4 = (bf16[64,3072]{1,0:T(8,128)(2,1)S(1)}, bf16[64,3072]{1,0:T(8,128)(2,1)}, u32[]{:S(2)}, u32[]{:S(2)}) collective-permute-start(bf16[64,3072]{1,0:T(8,128)(2,1)S(1)} %get-tuple-element.9), channel_id=1, source_target_pairs={{0,2},{1,3},{2,0},{3,1},{4,6},{5,7},{6,4},{7,5},{8,10},{9,11},{10,... | collective-permute-start | bytes 1179656 | tf_op jit(solution)/shard_map/ppermute | solution.py:30
  118.8 95.5 %all-gather.3.cloned.1.call-start = ((), (), s32[]{:S(2)}) async-start(), calls=%async_computation.4 | async-start | bytes 2949120 | tf_op jit(solution)/shard_map/all_gather | solution.py:98
  124.7 3.8 %copy-start.10 = (bf16[1,1024,1792]{2,1,0:T(8,128)(2,1)S(1)}, bf16[1,1024,1792]{2,1,0:T(8,128)(2,1)}, u32[]{:S(2)}) copy-start(bf16[1,1024,1792]{2,1,0:T(8,128)(2,1)} %param.13) | copy-start | bytes 11010052
  128.5 2.2 copy-start.12
  133.2 24.5 %collective-permute-start = (bf16[96,3072]{1,0:T(8,128)(2,1)S(1)}, bf16[96,3072]{1,0:T(8,128)(2,1)S(1)}, u32[]{:S(2)}, u32[]{:S(2)}) collective-permute-start(bf16[96,3072]{1,0:T(8,128)(2,1)S(1)} %get-tuple-element.4), channel_id=1, source_target_pairs={{0,1},{1,2},{2,3},{3,0},{4,5},{5,6},{6,7},{7,4},{8,9},{9,10},{10,1... | collective-permute-start | bytes 1769480 | tf_op jit(solution)/shard_map/ppermute | solution.py:30
  133.6 24.1 %collective-permute-start.2 = (bf16[96,3072]{1,0:T(8,128)(2,1)S(1)}, bf16[96,3072]{1,0:T(8,128)(2,1)S(1)}, u32[]{:S(2)}, u32[]{:S(2)}) collective-permute-start(bf16[96,3072]{1,0:T(8,128)(2,1)S(1)} %get-tuple-element.5), channel_id=1, source_target_pairs={{0,3},{1,0},{2,1},{3,2},{4,7},{5,4},{6,5},{7,6},{8,11},{9,8},{10,9... | collective-permute-start | bytes 1769480 | tf_op jit(solution)/shard_map/ppermute | solution.py:30
  136.0 34.7 %collective-permute-start.1 = (bf16[96,3072]{1,0:T(8,128)(2,1)S(1)}, bf16[96,3072]{1,0:T(8,128)(2,1)S(1)}, u32[]{:S(2)}, u32[]{:S(2)}) collective-permute-start(bf16[96,3072]{1,0:T(8,128)(2,1)S(1)} %get-tuple-element.6), channel_id=1, source_target_pairs={{0,2},{1,3},{2,0},{3,1},{4,6},{5,7},{6,4},{7,5},{8,10},{9,11},{10,... | collective-permute-start | bytes 1769480 | tf_op jit(solution)/shard_map/ppermute | solution.py:30
  176.6 3.5 %copy-start.13 = (bf16[1,1792,1024]{2,1,0:T(8,128)(2,1)S(1)}, bf16[1,1792,1024]{2,1,0:T(8,128)(2,1)}, u32[]{:S(2)}) copy-start(bf16[1,1792,1024]{2,1,0:T(8,128)(2,1)} %param.11) | copy-start | bytes 11010052
  183.6 39.7 %all-to-all-start.3 = ((bf16[128,2,1792]{2,1,0:T(2,128)(2,1)}), bf16[128,2,1792]{2,1,0:T(2,128)(2,1)S(1)}, u32[]{:S(2)}, u32[]{:S(2)}) async-start(bf16[128,2,1792]{2,1,0:T(2,128)(2,1)} %reshape.100), calls=%async_computation.3 | async-start | bytes 1835008 | tf_op jit(solution)/shard_map/all_to_all | solution.py:111
  214.4 4.1 %copy-start.14 = (bf16[1,1792,1024]{2,1,0:T(8,128)(2,1)S(1)}, bf16[1,1792,1024]{2,1,0:T(8,128)(2,1)}, u32[]{:S(2)}) copy-start(bf16[1,1792,1024]{2,1,0:T(8,128)(2,1)} %param.11) | copy-start | bytes 11010052
  223.3 36.4 %all-to-all-start.1 = ((bf16[128,3,1792]{2,1,0:T(4,128)(2,1)}), bf16[128,3,1792]{2,1,0:T(4,128)(2,1)S(1)}, u32[]{:S(2)}, u32[]{:S(2)}) async-start(bf16[128,3,1792]{2,1,0:T(4,128)(2,1)} %reshape.95), calls=%async_computation.1 | async-start | bytes 3670016 | tf_op jit(solution)/shard_map/all_to_all | solution.py:111
  232.1 3.3 %copy-start.2 = (bf16[384,3072]{1,0:T(8,128)(2,1)S(1)}, bf16[384,3072]{1,0:T(8,128)(2,1)}, u32[]{:S(2)}) copy-start(bf16[384,3072]{1,0:T(8,128)(2,1)} %all-gather.3.cloned.1.call-done) | copy-start | bytes 7077892
  235.4 1.3 copy-start.4
  235.4 1.6 copy-start.6
  241.6 4.5 %copy-start.3 = (bf16[384,1792]{1,0:T(8,128)(2,1)S(1)}, bf16[384,1792]{1,0:T(8,128)(2,1)}, u32[]{:S(2)}) copy-start(bf16[384,1792]{1,0:T(8,128)(2,1)} %get-tuple-element.10) | copy-start | bytes 4128772
  241.6 4.5 %copy-start.5 = (bf16[256,1792]{1,0:T(8,128)(2,1)S(1)}, bf16[256,1792]{1,0:T(8,128)(2,1)}, u32[]{:S(2)}) copy-start(bf16[256,1792]{1,0:T(8,128)(2,1)} %get-tuple-element.15) | copy-start | bytes 2752516
  250.6 10.4 %copy-start.1 = (bf16[4,32,2,1792]{3,0,2,1:T(4,128)(2,1)S(1)}, bf16[4,32,2,1792]{3,0,2,1:T(4,128)(2,1)}, u32[]{:S(2)}) copy-start(bf16[4,32,2,1792]{3,0,2,1:T(4,128)(2,1)} %copy.61) | copy-start | bytes 2752516
Sparse Core Ops, SparseCore 0:
  119.0 33.8 all-gather.4
  172.2 42.1 all-gather.2
where the time goes:
time: 271 us
  waiting for transfers between devices  130 us (48%)
  starting transfers between devices  41.8 us (15%)
  matrix products  41.3 us (15%)
  local copies, waits for them, and re-layouts  35.9 us (13%)
  between operations  14.6 us (5%)
  other arithmetic  6.6 us (2%)
    ppermute x6, waiting for transfers between devices, exchange(): came = lax.ppermute(block.astype(jnp.bfloat16), 'dp', pairs)  76.7 us
    all_gather x2, waiting for transfers between devices, shards(): lax.all_gather(jnp.concatenate([grad_pre, grad_lin, activated], axis=1),...  22.7 us
    all_to_all x2, waiting for transfers between devices, shards(): lax.all_to_all(flat_both, axes, split_axis=0, concat_axis=0, tiled=True)  21.8 us
    all_to_all x2, starting transfers between devices, shards(): lax.all_to_all(flat_both, axes, split_axis=0, concat_axis=0, tiled=True)  17.6 us
    all_to_all x2, starting transfers between devices, shards(): lax.all_to_all(flat_back, axes, split_axis=0, concat_axis=0, tiled=True)  16.9 us
    dot_general x3, matrix products, contract_rows(): lax.dot_general(left, right, (((0,), (0,)), ((), ())), preferred_element_...  13.6 us
    reshape x2, local copies, waits for them, and re-layouts, shards(): recv_both = recv_both.reshape(num_exp * num_dp * take, 2 * slice_width)  9.71 us
    all_to_all x2, waiting for transfers between devices, shards(): lax.all_to_all(flat_back, axes, split_axis=0, concat_axis=0, tiled=True)  9.12 us
  transfers between devices with their start and end apart: 12, of which 7 were waited for; matrix products, arithmetic and copies ran while one was open for 26% of the time, Pallas kernels for 0%

commit v1 on v0

--- a/solution.py
+++ b/solution.py
@@ -95,9 +95,13 @@
         grad_pre, grad_lin, activated = swiglu_back(
             summed[:, :hidden], summed[:, hidden : 2 * hidden], summed[:, 2 * hidden :]
         )
-        gathered = lax.all_gather(
-            jnp.concatenate([grad_pre, grad_lin, activated], axis=1), "dp", axis=0, tiled=True
+        part_sources_all_now = lambda inp: jnp.concatenate(
+            jax.lax.all_to_all(
+                jnp.stack([inp] * jax.lax.axis_size("dp")), "dp", split_axis=0, concat_axis=0
+            ),
+            axis=0,
         )
+        gathered = part_sources_all_now(jnp.concatenate([grad_pre, grad_lin, activated], axis=1))
         grad_pre = gathered[:, :hidden]
         grad_lin = gathered[:, hidden : 2 * hidden]
         activated = gathered[:, 2 * hidden :]

time: 271 us -> 254 us (0.937)
  waiting for transfers between devices: 130 us -> 113 us
  between operations: 14.6 us -> 1.2 us
  local copies, waits for them, and re-layouts: 35.9 us -> 43.6 us
  starting transfers between devices: 41.8 us -> 48 us
    ppermute x6, waiting for transfers between devices: 76.7 us -> 16.4 us  [exchange(): came = lax.ppermute(block.astype(jnp.bfloat16), 'dp', pairs)]
    all_to_all x0 -> x2, waiting for transfers between devices: none -> 29 us  [shards(): jax.lax.all_to_all(jnp.stack([inp] * jax.lax.axis_size('dp')), 'dp', spli...]
    all_to_all x2, waiting for transfers between devices: 21.8 us -> 50.2 us  [shards(): lax.all_to_all(flat_both, axes, split_axis=0, concat_axis=0, tiled=True)]
    all_gather x2 -> x0, waiting for transfers between devices: 22.7 us -> none  [shards(): lax.all_gather(jnp.concatenate([grad_pre, grad_lin, activated], axis=1),...]
    all_to_all x0 -> x2, starting transfers between devices: none -> 8.85 us  [shards(): jax.lax.all_to_all(jnp.stack([inp] * jax.lax.axis_size('dp')), 'dp', spli...]
    all_to_all x2, waiting for transfers between devices: 9.12 us -> 17.5 us  [shards(): lax.all_to_all(flat_back, axes, split_axis=0, concat_axis=0, tiled=True)]
    another operation x0 -> x2, local copies, waits for them, and re-layouts: none -> 3.01 us  [shards(): jnp.stack([inp] * jax.lax.axis_size('dp'))]
    unnamed x32 -> x36, local copies, waits for them, and re-layouts: 4.45 us -> 6.24 us
  transfers between devices with their start and end apart: 12 -> 12, of which waited for: 7 -> 8; matrix products, arithmetic and copies ran while one was open for 26% -> 30% of each run, Pallas kernels for 0% -> 0%
where the time goes in v1:
time: 254 us; the launch traced here: 253 us
  waiting for transfers between devices  113 us (44%)
  starting transfers between devices  48 us (19%)
  local copies, waits for them, and re-layouts  43.6 us (17%)
  matrix products  40.3 us (16%)
  other arithmetic  7.01 us (3%)
    all_to_all x2, waiting for transfers between devices, shards(): lax.all_to_all(flat_both, axes, split_axis=0, concat_axis=0, tiled=True)  50.2 us
    all_to_all x2, waiting for transfers between devices, shards(): jax.lax.all_to_all(jnp.stack([inp] * jax.lax.axis_size('dp')), 'dp', spli...  29 us
    all_to_all x2, starting transfers between devices, shards(): lax.all_to_all(flat_both, axes, split_axis=0, concat_axis=0, tiled=True)  17.6 us
    all_to_all x2, waiting for transfers between devices, shards(): lax.all_to_all(flat_back, axes, split_axis=0, concat_axis=0, tiled=True)  17.5 us
    ppermute x6, waiting for transfers between devices, exchange(): came = lax.ppermute(block.astype(jnp.bfloat16), 'dp', pairs)  16.4 us
    all_to_all x2, starting transfers between devices, shards(): lax.all_to_all(flat_back, axes, split_axis=0, concat_axis=0, tiled=True)  14.5 us
    dot_general x3, matrix products, contract_rows(): lax.dot_general(left, right, (((0,), (0,)), ((), ())), preferred_element_...  13.6 us
    reshape x2, local copies, waits for them, and re-layouts, shards(): recv_both = recv_both.reshape(num_exp * num_dp * take, 2 * slice_width)  9.71 us
  transfers between devices with their start and end apart: 12, of which 8 were waited for; matrix products, arithmetic and copies ran while one was open for 30% of the time, Pallas kernels for 0%

profile of v1, /device:TPU:1, one launch (start us, length us, event | category | flops | bytes accessed | tf_op | source)
XLA Modules:
  0.0 253.3 jit_solution(77656667332491750)
XLA Ops:
  4.6 1.6 reshape.108
  6.2 11.9 %all-to-all-start.3 = ((bf16[128,2,3584]{2,1,0:T(2,128)(2,1)}), bf16[128,2,3584]{2,1,0:T(2,128)(2,1)}, u32[]{:S(2)}, u32[]{:S(2)}) async-start(bf16[128,2,3584]{2,1,0:T(2,128)(2,1)} %reshape.108), calls=%async_computation.3 | async-start | bytes 3670016 | tf_op jit(solution)/shard_map/all_to_all | solution.py:85
  19.6 4.0 %reshape.102 = bf16[128,3,3584]{2,1,0:T(4,128)(2,1)} reshape(bf16[4,96,3584]{2,1,0:T(8,128)(2,1)S(1)} %fusion) | data formatting | bytes 5505024 | tf_op jit(solution)/shard_map/reshape | solution.py:84
  23.6 21.9 %all-to-all-done.3 = bf16[128,2,3584]{2,1,0:T(2,128)(2,1)} async-done(((bf16[128,2,3584]{2,1,0:T(2,128)(2,1)}), bf16[128,2,3584]{2,1,0:T(2,128)(2,1)}, u32[]{:S(2)}, u32[]{:S(2)}) %all-to-all-start.3) | async-done | bytes 1835040 | tf_op jit(solution)/shard_map/all_to_all | solution.py:85
  45.5 5.7 %all-to-all-start = ((bf16[128,3,3584]{2,1,0:T(4,128)(2,1)}), bf16[128,3,3584]{2,1,0:T(4,128)(2,1)}, u32[]{:S(2)}, u32[]{:S(2)}) async-start(bf16[128,3,3584]{2,1,0:T(4,128)(2,1)} %reshape.102), calls=%async_computation | async-start | bytes 7340032 | tf_op jit(solution)/shard_map/all_to_all | solution.py:85
  51.2 4.1 %reshape.109 = bf16[256,3584]{1,0:T(8,128)(2,1)S(1)} reshape(bf16[128,2,3584]{2,1,0:T(2,128)(2,1)} %all-to-all-done.3) | data formatting | bytes 3670016 | tf_op jit(solution)/shard_map/reshape | solution.py:86
  55.3 3.8 %fusion.8 = f32[256,1024]{1,0:T(8,128)S(1)} fusion(bf16[1,1792,1024]{2,1,0:T(8,128)(2,1)} %param.12, bf16[256,3584]{1,0:T(8,128)(2,1)S(1)} %reshape.109), kind=kOutput, calls=%fused_computation.14 | convolution fusion | flops 939524096 | bytes 5636096 | tf_op jit(solution)/shard_map/dot_general | solution.py:90
  62.8 1.7 copy-done.1
  65.6 1.4 collective-permute-start.3
  66.9 1.3 collective-permute-start.5
  68.2 1.7 collective-permute-start.4
  69.9 28.4 %all-to-all-done = bf16[128,3,3584]{2,1,0:T(4,128)(2,1)} async-done(((bf16[128,3,3584]{2,1,0:T(4,128)(2,1)}), bf16[128,3,3584]{2,1,0:T(4,128)(2,1)}, u32[]{:S(2)}, u32[]{:S(2)}) %all-to-all-start) | async-done | bytes 2752544 | tf_op jit(solution)/shard_map/all_to_all | solution.py:85
  98.3 5.6 %reshape.103 = bf16[384,3584]{1,0:T(8,128)(2,1)S(1)} reshape(bf16[128,3,3584]{2,1,0:T(4,128)(2,1)} %all-to-all-done) | data formatting | bytes 5505024 | tf_op jit(solution)/shard_map/reshape | solution.py:86
  103.9 3.8 %fusion.12 = f32[384,1024]{1,0:T(8,128)S(1)} fusion(bf16[1,1792,1024]{2,1,0:T(8,128)(2,1)} %param.12, bf16[384,3584]{1,0:T(8,128)(2,1)S(1)} %reshape.103), kind=kOutput, calls=%fused_computation.18 | convolution fusion | flops 1409286144 | bytes 6619136 | tf_op jit(solution)/shard_map/dot_general | solution.py:90
  107.7 1.6 fusion.4
  109.8 1.7 fusion.20
  112.0 1.5 fusion.57
  113.8 2.3 collective-permute-start.2
  116.2 1.7 fusion.56
  118.0 1.3 stack.5
  119.3 4.4 %all-to-all-start.4 = ((bf16[4,64,3072]{2,1,0:T(8,128)(2,1)}), bf16[4,64,3072]{2,1,0:T(8,128)(2,1)}, u32[]{:S(2)}, u32[]{:S(2)}) async-start(bf16[4,64,3072]{2,1,0:T(8,128)(2,1)} %stack.5), calls=%async_computation.4 | async-start | bytes 3145728 | tf_op jit(solution)/shard_map/all_to_all | solution.py:99
  123.7 4.8 %collective-permute-done = bf16[96,3072]{1,0:T(8,128)(2,1)S(1)} collective-permute-done((bf16[96,3072]{1,0:T(8,128)(2,1)}, bf16[96,3072]{1,0:T(8,128)(2,1)S(1)}, u32[]{:S(2)}, u32[]{:S(2)}) %collective-permute-start) | collective-permute-done | bytes 589856 | tf_op jit(solution)/shard_map/ppermute | solution.py:30
  128.5 11.6 %collective-permute-done.1 = bf16[96,3072]{1,0:T(8,128)(2,1)} collective-permute-done((bf16[96,3072]{1,0:T(8,128)(2,1)}, bf16[96,3072]{1,0:T(8,128)(2,1)}, u32[]{:S(2)}, u32[]{:S(2)}) %collective-permute-start.1) | collective-permute-done | bytes 589856 | tf_op jit(solution)/shard_map/ppermute | solution.py:30
  140.1 1.9 fusion.54
  142.3 14.7 %all-to-all-done.4 = bf16[4,64,3072]{2,1,0:T(8,128)(2,1)} async-done(((bf16[4,64,3072]{2,1,0:T(8,128)(2,1)}), bf16[4,64,3072]{2,1,0:T(8,128)(2,1)}, u32[]{:S(2)}, u32[]{:S(2)}) %all-to-all-start.4) | async-done | bytes 1572896 | tf_op jit(solution)/shard_map/all_to_all | solution.py:99
  157.0 1.7 stack.4
  158.7 4.5 %all-to-all-start.1 = ((bf16[4,96,3072]{2,1,0:T(8,128)(2,1)}), bf16[4,96,3072]{2,1,0:T(8,128)(2,1)}, u32[]{:S(2)}, u32[]{:S(2)}) async-start(bf16[4,96,3072]{2,1,0:T(8,128)(2,1)} %stack.4), calls=%async_computation.1 | async-start | bytes 4718592 | tf_op jit(solution)/shard_map/all_to_all | solution.py:99
  163.2 2.9 %fusion.87 = (bf16[256,1792]{1,0:T(8,128)(2,1)}, bf16[256,1792]{1,0:T(8,128)(2,1)}) fusion(bf16[256,3584]{1,0:T(8,128)(2,1)} %copy-done.2), kind=kLoop, calls=%fused_computation.114 | loop fusion | bytes 3670016 | tf_op jit(solution)/shard_map/slice | solution.py:88
  166.1 1.7 fusion.85
  167.8 1.3 copy-done.12
  169.2 2.4 fusion.6
  171.6 2.2 fusion.34
  175.1 14.3 %all-to-all-done.1 = bf16[4,96,3072]{2,1,0:T(8,128)(2,1)} async-done(((bf16[4,96,3072]{2,1,0:T(8,128)(2,1)}), bf16[4,96,3072]{2,1,0:T(8,128)(2,1)}, u32[]{:S(2)}, u32[]{:S(2)}) %all-to-all-start.1) | async-done | bytes 2359328 | tf_op jit(solution)/shard_map/all_to_all | solution.py:99
  189.3 9.8 %all-to-all-start.5 = ((bf16[128,2,1792]{2,1,0:T(2,128)(2,1)}), bf16[128,2,1792]{2,1,0:T(2,128)(2,1)S(1)}, u32[]{:S(2)}, u32[]{:S(2)}) async-start(bf16[128,2,1792]{2,1,0:T(2,128)(2,1)} %reshape.112), calls=%async_computation.5 | async-start | bytes 1835008 | tf_op jit(solution)/shard_map/all_to_all | solution.py:115
  199.2 4.1 %fusion.10 = f32[384,1792]{1,0:T(8,128)S(1)} fusion(bf16[1,1792,1024]{2,1,0:T(8,128)(2,1)} %param.12, bf16[384,3072]{1,0:T(8,128)(2,1)} %bitcast.11), kind=kOutput, calls=%fused_computation.16 | convolution fusion | flops 1409286144 | bytes 7208960 | tf_op jit(solution)/shard_map/dot_general | solution.py:110
  203.3 2.8 %fusion.28 = bf16[384,1792]{1,0:T(8,128)(2,1)S(1)} fusion(f32[384,1792]{1,0:T(8,128)S(1)} %fusion.10, bf16[1,1792,1024]{2,1,0:T(8,128)(2,1)S(1)} %copy-done.16, bf16[384,3072]{1,0:T(8,128)(2,1)} %bitcast.11), kind=kOutput, calls=%fused_computation.33 | convolution fusion | flops 1410662400 | bytes 8585216 | tf_op jit(solution)/shard_map/dot_general | solution.py:108
  206.1 2.1 reshape.106
  208.2 8.8 %all-to-all-done.5 = bf16[128,2,1792]{2,1,0:T(2,128)(2,1)S(1)} async-done(((bf16[128,2,1792]{2,1,0:T(2,128)(2,1)}), bf16[128,2,1792]{2,1,0:T(2,128)(2,1)S(1)}, u32[]{:S(2)}, u32[]{:S(2)}) %all-to-all-start.5) | async-done | bytes 917536 | tf_op jit(solution)/shard_map/all_to_all | solution.py:115
  217.0 4.6 %all-to-all-start.2 = ((bf16[128,3,1792]{2,1,0:T(4,128)(2,1)}), bf16[128,3,1792]{2,1,0:T(4,128)(2,1)S(1)}, u32[]{:S(2)}, u32[]{:S(2)}) async-start(bf16[128,3,1792]{2,1,0:T(4,128)(2,1)} %reshape.106), calls=%async_computation.2 | async-start | bytes 3670016 | tf_op jit(solution)/shard_map/all_to_all | solution.py:115
  221.7 1.5 fusion.88
  223.1 1.7 copy.61
  224.8 2.0 fusion.86
  227.1 4.5 %fusion.23 = bf16[1,1792,1024]{2,1,0:T(8,128)(2,1)} fusion(bf16[256,1792]{1,0:T(8,128)(2,1)S(1)} %copy-done.7, bf16[384,1792]{1,0:T(8,128)(2,1)S(1)} %copy-done.5, bf16[256,1024]{1,0:T(8,128)(2,1)S(1)} %get-tuple-element.18, bf16[384,1024]{1,0:T(8,128)(2,1)S(1)} %get-tuple-element.13), kind=kOutput, calls=%fused_computation.29 | convolution fusion | flops 2357854208 | bytes 7274496 | tf_op jit(solution)/shard_map/dot_general | solution.py:17
  231.6 4.5 %fusion.22 = bf16[1,1792,1024]{2,1,0:T(8,128)(2,1)} fusion(bf16[256,1792]{1,0:T(8,128)(2,1)S(1)} %copy-done.7, bf16[384,1792]{1,0:T(8,128)(2,1)S(1)} %copy-done.5, bf16[256,1024]{1,0:T(8,128)(2,1)S(1)} %get-tuple-element.19, bf16[384,1024]{1,0:T(8,128)(2,1)S(1)} %get-tuple-element.14), kind=kOutput, calls=%fused_computation.28 | convolution fusion | flops 2357854208 | bytes 7274496 | tf_op jit(solution)/shard_map/dot_general | solution.py:17
  236.2 4.5 %fusion.24 = bf16[1,1024,1792]{2,1,0:T(8,128)(2,1)} fusion(bf16[256,1792]{1,0:T(8,128)(2,1)S(1)} %copy-done.6, bf16[384,1792]{1,0:T(8,128)(2,1)S(1)} %copy-done.4, bf16[256,1024]{1,0:T(8,128)(2,1)S(1)} %get-tuple-element.17, bf16[384,1024]{1,0:T(8,128)(2,1)S(1)} %get-tuple-element.12), kind=kOutput, calls=%fused_computation.30 | convolution fusion | flops 2357854208 | bytes 7274496 | tf_op jit(solution)/shard_map/dot_general | solution.py:17
  240.7 8.7 %all-to-all-done.2 = bf16[128,3,1792]{2,1,0:T(4,128)(2,1)S(1)} async-done(((bf16[128,3,1792]{2,1,0:T(4,128)(2,1)}), bf16[128,3,1792]{2,1,0:T(4,128)(2,1)S(1)}, u32[]{:S(2)}, u32[]{:S(2)}) %all-to-all-start.2) | async-done | bytes 1376288 | tf_op jit(solution)/shard_map/all_to_all | solution.py:115
  249.4 1.3 copy.60
  250.7 1.5 pad_maximum_fusion.2
  (79 shorter events, 14.4 us)
Async XLA Ops:
  0.6 3.2 %copy-start.8 = (bf16[16,7168]{1,0:T(8,128)(2,1)S(1)}, bf16[16,7168]{1,0:T(8,128)(2,1)}, u32[]{:S(2)}) copy-start(bf16[16,7168]{1,0:T(8,128)(2,1)} %param.8) | copy-start | bytes 688132
  0.6 3.2 %copy-start.9 = (bf16[16,7168]{1,0:T(8,128)(2,1)S(1)}, bf16[16,7168]{1,0:T(8,128)(2,1)}, u32[]{:S(2)}) copy-start(bf16[16,7168]{1,0:T(8,128)(2,1)} %param.7) | copy-start | bytes 688132
  6.2 39.2 %all-to-all-start.3 = ((bf16[128,2,3584]{2,1,0:T(2,128)(2,1)}), bf16[128,2,3584]{2,1,0:T(2,128)(2,1)}, u32[]{:S(2)}, u32[]{:S(2)}) async-start(bf16[128,2,3584]{2,1,0:T(2,128)(2,1)} %reshape.108), calls=%async_computation.3 | async-start | bytes 3670016 | tf_op jit(solution)/shard_map/all_to_all | solution.py:85
  45.5 52.8 %all-to-all-start = ((bf16[128,3,3584]{2,1,0:T(4,128)(2,1)}), bf16[128,3,3584]{2,1,0:T(4,128)(2,1)}, u32[]{:S(2)}, u32[]{:S(2)}) async-start(bf16[128,3,3584]{2,1,0:T(4,128)(2,1)} %reshape.102), calls=%async_computation | async-start | bytes 7340032 | tf_op jit(solution)/shard_map/all_to_all | solution.py:85
  55.3 5.0 %copy-start.2 = (bf16[256,3584]{1,0:T(8,128)(2,1)}, bf16[256,3584]{1,0:T(8,128)(2,1)S(1)}, u32[]{:S(2)}) copy-start(bf16[256,3584]{1,0:T(8,128)(2,1)S(1)} %reshape.109) | copy-start | bytes 5505028
  55.3 3.9 %copy-start.10 = (bf16[1,1024,1792]{2,1,0:T(8,128)(2,1)S(1)}, bf16[1,1024,1792]{2,1,0:T(8,128)(2,1)}, u32[]{:S(2)}) copy-start(bf16[1,1024,1792]{2,1,0:T(8,128)(2,1)} %param.13) | copy-start | bytes 11010052
  59.2 2.0 copy-start.13
  62.8 1.7 copy-start.1
  65.6 50.6 %collective-permute-start.3 = (bf16[64,3072]{1,0:T(8,128)(2,1)}, bf16[64,3072]{1,0:T(8,128)(2,1)}, u32[]{:S(2)}, u32[]{:S(2)}) collective-permute-start(bf16[64,3072]{1,0:T(8,128)(2,1)} %get-tuple-element.7), channel_id=1, source_target_pairs={{0,1},{1,2},{2,3},{3,0},{4,5},{5,6},{6,7},{7,4},{8,9},{9,10},{10,1... | collective-permute-start | bytes 1179656 | tf_op jit(solution)/shard_map/ppermute | solution.py:30
  66.9 49.2 %collective-permute-start.5 = (bf16[64,3072]{1,0:T(8,128)(2,1)}, bf16[64,3072]{1,0:T(8,128)(2,1)}, u32[]{:S(2)}, u32[]{:S(2)}) collective-permute-start(bf16[64,3072]{1,0:T(8,128)(2,1)} %get-tuple-element.8), channel_id=1, source_target_pairs={{0,3},{1,0},{2,1},{3,2},{4,7},{5,4},{6,5},{7,6},{8,11},{9,8},{10,9... | collective-permute-start | bytes 1179656 | tf_op jit(solution)/shard_map/ppermute | solution.py:30
  68.2 47.9 %collective-permute-start.4 = (bf16[64,3072]{1,0:T(8,128)(2,1)}, bf16[64,3072]{1,0:T(8,128)(2,1)}, u32[]{:S(2)}, u32[]{:S(2)}) collective-permute-start(bf16[64,3072]{1,0:T(8,128)(2,1)} %get-tuple-element.9), channel_id=1, source_target_pairs={{0,2},{1,3},{2,0},{3,1},{4,6},{5,7},{6,4},{7,5},{8,10},{9,11},{10,... | collective-permute-start | bytes 1179656 | tf_op jit(solution)/shard_map/ppermute | solution.py:30
  103.9 3.8 %copy-start.11 = (bf16[1,1024,1792]{2,1,0:T(8,128)(2,1)S(1)}, bf16[1,1024,1792]{2,1,0:T(8,128)(2,1)}, u32[]{:S(2)}) copy-start(bf16[1,1024,1792]{2,1,0:T(8,128)(2,1)} %param.13) | copy-start | bytes 11010052
  107.7 2.0 copy-start.14
  112.0 5.9 %copy-start = (f32[384,3072]{1,0:T(8,128)}, f32[384,3072]{1,0:T(8,128)S(1)}, u32[]{:S(2)}) copy-start(f32[384,3072]{1,0:T(8,128)S(1)} %pad_maximum_fusion) | copy-start | bytes 14155780
  113.5 15.1 %collective-permute-start = (bf16[96,3072]{1,0:T(8,128)(2,1)}, bf16[96,3072]{1,0:T(8,128)(2,1)S(1)}, u32[]{:S(2)}, u32[]{:S(2)}) collective-permute-start(bf16[96,3072]{1,0:T(8,128)(2,1)} %get-tuple-element.4), channel_id=1, source_target_pairs={{0,1},{1,2},{2,3},{3,0},{4,5},{5,6},{6,7},{7,4},{8,9},{9,10},{10,1... | collective-permute-start | bytes 1769480 | tf_op jit(solution)/shard_map/ppermute | solution.py:30
  113.8 14.7 %collective-permute-start.2 = (bf16[96,3072]{1,0:T(8,128)(2,1)}, bf16[96,3072]{1,0:T(8,128)(2,1)}, u32[]{:S(2)}, u32[]{:S(2)}) collective-permute-start(bf16[96,3072]{1,0:T(8,128)(2,1)} %get-tuple-element.5), channel_id=1, source_target_pairs={{0,3},{1,0},{2,1},{3,2},{4,7},{5,4},{6,5},{7,6},{8,11},{9,8},{10,9... | collective-permute-start | bytes 1769480 | tf_op jit(solution)/shard_map/ppermute | solution.py:30
  116.1 24.0 %collective-permute-start.1 = (bf16[96,3072]{1,0:T(8,128)(2,1)}, bf16[96,3072]{1,0:T(8,128)(2,1)}, u32[]{:S(2)}, u32[]{:S(2)}) collective-permute-start(bf16[96,3072]{1,0:T(8,128)(2,1)} %get-tuple-element.6), channel_id=1, source_target_pairs={{0,2},{1,3},{2,0},{3,1},{4,6},{5,7},{6,4},{7,5},{8,10},{9,11},{10,... | collective-permute-start | bytes 1769480 | tf_op jit(solution)/shard_map/ppermute | solution.py:30
  119.3 37.7 %all-to-all-start.4 = ((bf16[4,64,3072]{2,1,0:T(8,128)(2,1)}), bf16[4,64,3072]{2,1,0:T(8,128)(2,1)}, u32[]{:S(2)}, u32[]{:S(2)}) async-start(bf16[4,64,3072]{2,1,0:T(8,128)(2,1)} %stack.5), calls=%async_computation.4 | async-start | bytes 3145728 | tf_op jit(solution)/shard_map/all_to_all | solution.py:99
  158.7 30.6 %all-to-all-start.1 = ((bf16[4,96,3072]{2,1,0:T(8,128)(2,1)}), bf16[4,96,3072]{2,1,0:T(8,128)(2,1)}, u32[]{:S(2)}, u32[]{:S(2)}) async-start(bf16[4,96,3072]{2,1,0:T(8,128)(2,1)} %stack.4), calls=%async_computation.1 | async-start | bytes 4718592 | tf_op jit(solution)/shard_map/all_to_all | solution.py:99
  166.1 3.0 %copy-start.12 = (bf16[1,1792,1024]{2,1,0:T(8,128)(2,1)S(1)}, bf16[1,1792,1024]{2,1,0:T(8,128)(2,1)}, u32[]{:S(2)}) copy-start(bf16[1,1792,1024]{2,1,0:T(8,128)(2,1)} %param.12) | copy-start | bytes 11010052
  169.2 2.4 copy-start.15
  189.3 27.7 %all-to-all-start.5 = ((bf16[128,2,1792]{2,1,0:T(2,128)(2,1)}), bf16[128,2,1792]{2,1,0:T(2,128)(2,1)S(1)}, u32[]{:S(2)}, u32[]{:S(2)}) async-start(bf16[128,2,1792]{2,1,0:T(2,128)(2,1)} %reshape.112), calls=%async_computation.5 | async-start | bytes 1835008 | tf_op jit(solution)/shard_map/all_to_all | solution.py:115
  199.2 4.1 %copy-start.16 = (bf16[1,1792,1024]{2,1,0:T(8,128)(2,1)S(1)}, bf16[1,1792,1024]{2,1,0:T(8,128)(2,1)}, u32[]{:S(2)}) copy-start(bf16[1,1792,1024]{2,1,0:T(8,128)(2,1)} %param.11) | copy-start | bytes 11010052
  217.0 32.4 %all-to-all-start.2 = ((bf16[128,3,1792]{2,1,0:T(4,128)(2,1)}), bf16[128,3,1792]{2,1,0:T(4,128)(2,1)S(1)}, u32[]{:S(2)}, u32[]{:S(2)}) async-start(bf16[128,3,1792]{2,1,0:T(4,128)(2,1)} %reshape.106), calls=%async_computation.2 | async-start | bytes 3670016 | tf_op jit(solution)/shard_map/all_to_all | solution.py:115
  224.8 2.1 copy-start.5
  224.8 2.3 copy-start.7
  231.6 4.5 %copy-start.4 = (bf16[384,1792]{1,0:T(8,128)(2,1)S(1)}, bf16[384,1792]{1,0:T(8,128)(2,1)}, u32[]{:S(2)}) copy-start(bf16[384,1792]{1,0:T(8,128)(2,1)} %get-tuple-element.10) | copy-start | bytes 4128772
  231.6 4.5 %copy-start.6 = (bf16[256,1792]{1,0:T(8,128)(2,1)S(1)}, bf16[256,1792]{1,0:T(8,128)(2,1)}, u32[]{:S(2)}) copy-start(bf16[256,1792]{1,0:T(8,128)(2,1)} %get-tuple-element.15) | copy-start | bytes 2752516
  240.7 10.0 %copy-start.3 = (bf16[4,32,2,1792]{3,0,2,1:T(4,128)(2,1)S(1)}, bf16[4,32,2,1792]{3,0,2,1:T(4,128)(2,1)}, u32[]{:S(2)}) copy-start(bf16[4,32,2,1792]{3,0,2,1:T(4,128)(2,1)} %copy.61) | copy-start | bytes 2752516
